TPU v7x, 256 devices: a whole 4x4x8 slice. The times are simulated.
256 devices in a mesh: blk: 8 (over y, x_hi), grp: 32 (over x_lo, z, core).
Axes of the slice: x: 4 (x_hi: 2, x_lo: 2; x = x_hi * 2 + x_lo), y: 4, z: 8, core: 2. Of those that a mesh axis runs over, the one named last changes fastest.
Arguments:
- position: float32 [3, 65536], P(None, ('blk', 'grp'))
- velocity: float32 [3, 65536], P(None, ('blk', 'grp')), may hold values from -3 to 3
- accel_old: float32 [3, 65536], P(None, ('blk', 'grp')), may hold values from -5 to 5
- jerk_old: float32 [3, 65536], P(None, ('blk', 'grp')), may hold values from -5 to 5
- elapsed: float32 [65536], P(('blk', 'grp')), may hold values from 0.01 to 0.1
- masses: float32 [65536], P(('blk', 'grp'))
- active_stars: int32 [8192], P(('blk', 'grp')), may hold values from 0 to 255, as said below
- neighbour_list: int32 [256, 64], P(('blk', 'grp')), may hold values from 0 to 63, as said below
- neighbour_count: int32 [256], P(('blk', 'grp')), may hold values from 1 to 64, as said below
Outputs:
- regular: float32 [6, 8192], P(None, ('blk', 'grp'))
- irregular: float32 [6, 8192], P(None, ('blk', 'grp'))
- correction: float32 [6, 8192], P(None, ('blk', 'grp'))
Inputs may be any that keep to these rules, and one draw needn't show every extreme that they name: `active_stars`: the 32 entries of one device are distinct local indices of that device's stars, all inside one block of 128 of them. `neighbour_list`: row r lists neighbour blocks for the active stars of device r, numbered within r's group (2 blocks a device, devices in grp order). Its first neighbour_count[r] entries are distinct and ascending, at most 2 of them from one device, and include the block that holds r's active stars; later entries mean nothing. `neighbour_count`: in every group along blk some device lists 2 blocks of every device of its group.
All inputs are finite; a program needn't handle non-finite values.
Results may differ from a plain program's by a relative error of at most 0.0003.
Values sent between devices are 32-bit elements; how exact they have to be, the bound alone decides.
No kernel may reach another device: no remote copies, remote signals or barrier semaphores. Data moves between devices by JAX's collectives and lax.ppermute only.
A program may use at most 64 MiB of HBM per device.

v0:
```python
import jax
import jax.numpy as jnp
from jax import lax
from jax.sharding import PartitionSpec as P

BLOCK = 128
soften_sq = 0.0001


def pair_sums(targets, sources, weight):
    gap_x = sources[0][None, :] - targets[0][:, None]
    gap_y = sources[1][None, :] - targets[1][:, None]
    gap_z = sources[2][None, :] - targets[2][:, None]
    rel_x = sources[3][None, :] - targets[3][:, None]
    rel_y = sources[4][None, :] - targets[4][:, None]
    rel_z = sources[5][None, :] - targets[5][:, None]
    dist_sq = gap_x * gap_x + gap_y * gap_y + gap_z * gap_z + soften_sq
    inverse = lax.rsqrt(dist_sq)
    scaled = weight * (inverse * inverse * inverse)
    radial = 3.0 * (gap_x * rel_x + gap_y * rel_y + gap_z * rel_z) / dist_sq
    term_list = [
        gap_x,
        gap_y,
        gap_z,
        rel_x - radial * gap_x,
        rel_y - radial * gap_y,
        rel_z - radial * gap_z,
    ]
    return jnp.stack([jnp.sum(scaled * term, axis=1) for term in term_list])


def per_device(
    position,
    velocity,
    accel_old,
    jerk_old,
    elapsed,
    masses,
    active_stars,
    neighbour_list,
    neighbour_count,
):
    moved_pos = position + elapsed * (
        velocity + elapsed * (0.5 * accel_old + elapsed * jerk_old / 6.0)
    )
    turned = velocity + elapsed * (accel_old + 0.5 * elapsed * jerk_old)
    sources = jnp.concatenate([moved_pos, turned], axis=0)
    own_set = jnp.take(sources, active_stars, axis=1)
    act_dev = active_stars.shape[0]
    block_data = jnp.concatenate([sources, masses[None, :]], axis=0)
    group = lax.all_gather(block_data, "grp", axis=1, tiled=True)
    group_src = group[:6]
    group_mass = group[6]
    targets = lax.all_gather(own_set, "blk", axis=1, tiled=True)
    blk_size = lax.axis_size("blk")
    blk_here = lax.axis_index("blk")
    block_total = group_src.shape[1] // BLOCK
    slot_total = neighbour_list.shape[1]
    own_live = jnp.arange(slot_total) < neighbour_count[0]
    near = jnp.any(
        own_live[:, None] & (neighbour_list[0][:, None] == jnp.arange(block_total)[None, :]), axis=0
    ).astype(jnp.float32)
    owner_rows = jnp.arange(blk_size)
    keep = jnp.where((owner_rows == blk_here)[:, None], 1.0 - near[None, :], 1.0)
    target_pieces = targets.reshape(6, blk_size, act_dev).transpose(1, 0, 2)

    def one_piece(items):
        target_piece, keep_piece = items
        weight = jnp.repeat(keep_piece, BLOCK)[None, :] * group_mass[None, :]
        return pair_sums(target_piece, group_src, weight)

    sums = lax.map(one_piece, (target_pieces, keep))
    partial_terms = sums.transpose(1, 0, 2).reshape(6, blk_size * act_dev)
    regular = lax.psum_scatter(partial_terms, "blk", scatter_dimension=1, tiled=True)
    near_mass = (jnp.repeat(near, BLOCK) * group_mass)[None, :]
    irregular = pair_sums(own_set, group_src, near_mass)
    accel_now = regular[:3] + irregular[:3]
    jerk_now = regular[3:] + irregular[3:]
    step_time = jnp.take(elapsed, active_stars)
    start_accel = jnp.take(accel_old, active_stars, axis=1)
    start_jerk = jnp.take(jerk_old, active_stars, axis=1)
    change = start_accel - accel_now
    snap_term = -6.0 * change - step_time * (4.0 * start_jerk + 2.0 * jerk_now)
    crackle_term = 12.0 * change + 6.0 * step_time * (start_jerk + jerk_now)
    return (regular, irregular, jnp.concatenate([snap_term, crackle_term], axis=0))


def solution(mesh):
    in_specs = (
        P(None, ("blk", "grp")),
        P(None, ("blk", "grp")),
        P(None, ("blk", "grp")),
        P(None, ("blk", "grp")),
        P(("blk", "grp")),
        P(("blk", "grp")),
        P(("blk", "grp")),
        P(("blk", "grp"), None),
        P(("blk", "grp")),
    )
    out_specs = (P(None, ("blk", "grp")), P(None, ("blk", "grp")), P(None, ("blk", "grp")))
    return jax.shard_map(
        per_device, mesh=mesh, in_specs=in_specs, out_specs=out_specs, check_vma=False
    )
```

profile of v0, /device:TPU:32, one launch (start us, length us, event | category | flops | bytes accessed | tf_op | source)
XLA Modules:
  0.0 184.2 jit_solution(8976956344711509726)
XLA Ops:
  7.9 0.8 fusion.42
  8.7 0.7 copy-done
  9.5 0.1 copy.108
  9.6 0.5 copy-done.7
  10.1 0.7 gather_fusion.1
  10.8 0.6 gather_fusion
  11.4 0.7 copy-done.6
  12.1 34.8 %all_gather.6 = f32[7,8192]{1,0:T(8,128)S(1)} all-gather(f32[7,256]{1,0:T(8,128)S(1)} %pad_maximum_fusion), channel_id=1, replica_groups=mesh['blk'=8,'grp'=32] {'grp'}, dimensions={1}, use_global_device_ids=true | all-gather | bytes 236544 | tf_op jit(solution)/shard_map/all_gather | solution.py:51
  47.0 0.1 copy.109
  47.1 34.6 %all-gather = f32[8,32,6]{1,2,0:T(8,128)S(1)} all-gather(f32[1,32,6]{1,2,0:T(8,128)S(1)} %copy.109), channel_id=1, replica_groups=mesh['blk'=8,'grp'=32] {'blk'}, dimensions={0}, use_global_device_ids=true | all-gather | bytes 6912 | tf_op jit(solution)/shard_map/all_gather | solution.py:54
  81.7 0.1 reshape.131
  81.8 0.1 reshape.91
  82.0 0.2 fusion.50
  82.2 18.5 %while.10 = (s32[]{:T(128)}, f32[8,6,32]{2,1,0:T(8,128)S(1)}, f32[8,64]{1,0:T(8,128)S(1)}, f32[1,8192]{1,0:T(1,128)S(1)}, f32[6,8192]{1,0:T(8,128)S(1)}, /*index...) while((s32[]{:T(128)}, f32[8,6,32]{2,1,0:T(8,128)S(1)}, ...), condition=%wide.region_8.9_spmd, body=%wide.region_1.8_spmd.sunk | while | flops 10493767 | bytes 701913 | solution.py:72
  82.2 0.1 fusion.56
  82.4 0.1 bitcast_multiply_fusion.3
  82.5 2.0 %fusion.58 = (f32[32]{0:T(128)S(1)}, f32[32]{0:T(128)S(1)}, f32[32]{0:T(128)S(1)}, f32[32]{0:T(128)S(1)}, f32[32]{0:T(128)S(1)}, /*index=5*/f32[32]{0:T(128)S(1)}) fusion(f32[32]{0:T(128)S(1)} %get-tuple-element.206, f32[8192]{0:T(1024)S(1)} %bitcast.131, f32[32]{0:T(128)S(1)} %get-tuple-element.208, f32[8192]{0:T(1024)S(1)} %bitcast.133, ...), kind=kLoop, calls=%fused_computation.25.clone.1 | loop fusion | flops 10485568 | bytes 230912 | tf_op jit(solution)/shard_map/while/body/eval_jaxpr/reduce_sum | solution.py:29
  84.6 0.1 fusion.56
  84.7 0.1 bitcast_multiply_fusion.3
  84.8 2.0 %fusion.58 = (f32[32]{0:T(128)S(1)}, f32[32]{0:T(128)S(1)}, f32[32]{0:T(128)S(1)}, f32[32]{0:T(128)S(1)}, f32[32]{0:T(128)S(1)}, /*index=5*/f32[32]{0:T(128)S(1)}) fusion(f32[32]{0:T(128)S(1)} %get-tuple-element.206, f32[8192]{0:T(1024)S(1)} %bitcast.131, f32[32]{0:T(128)S(1)} %get-tuple-element.208, f32[8192]{0:T(1024)S(1)} %bitcast.133, ...), kind=kLoop, calls=%fused_computation.25.clone.1 | loop fusion | flops 10485568 | bytes 230912 | tf_op jit(solution)/shard_map/while/body/eval_jaxpr/reduce_sum | solution.py:29
  86.9 0.1 fusion.56
  87.0 0.1 bitcast_multiply_fusion.3
  87.1 2.0 %fusion.58 = (f32[32]{0:T(128)S(1)}, f32[32]{0:T(128)S(1)}, f32[32]{0:T(128)S(1)}, f32[32]{0:T(128)S(1)}, f32[32]{0:T(128)S(1)}, /*index=5*/f32[32]{0:T(128)S(1)}) fusion(f32[32]{0:T(128)S(1)} %get-tuple-element.206, f32[8192]{0:T(1024)S(1)} %bitcast.131, f32[32]{0:T(128)S(1)} %get-tuple-element.208, f32[8192]{0:T(1024)S(1)} %bitcast.133, ...), kind=kLoop, calls=%fused_computation.25.clone.1 | loop fusion | flops 10485568 | bytes 230912 | tf_op jit(solution)/shard_map/while/body/eval_jaxpr/reduce_sum | solution.py:29
  89.2 0.1 fusion.56
  89.4 2.0 %fusion.58 = (f32[32]{0:T(128)S(1)}, f32[32]{0:T(128)S(1)}, f32[32]{0:T(128)S(1)}, f32[32]{0:T(128)S(1)}, f32[32]{0:T(128)S(1)}, /*index=5*/f32[32]{0:T(128)S(1)}) fusion(f32[32]{0:T(128)S(1)} %get-tuple-element.206, f32[8192]{0:T(1024)S(1)} %bitcast.131, f32[32]{0:T(128)S(1)} %get-tuple-element.208, f32[8192]{0:T(1024)S(1)} %bitcast.133, ...), kind=kLoop, calls=%fused_computation.25.clone.1 | loop fusion | flops 10485568 | bytes 230912 | tf_op jit(solution)/shard_map/while/body/eval_jaxpr/reduce_sum | solution.py:29
  91.5 0.1 fusion.56
  91.8 2.0 %fusion.58 = (f32[32]{0:T(128)S(1)}, f32[32]{0:T(128)S(1)}, f32[32]{0:T(128)S(1)}, f32[32]{0:T(128)S(1)}, f32[32]{0:T(128)S(1)}, /*index=5*/f32[32]{0:T(128)S(1)}) fusion(f32[32]{0:T(128)S(1)} %get-tuple-element.206, f32[8192]{0:T(1024)S(1)} %bitcast.131, f32[32]{0:T(128)S(1)} %get-tuple-element.208, f32[8192]{0:T(1024)S(1)} %bitcast.133, ...), kind=kLoop, calls=%fused_computation.25.clone.1 | loop fusion | flops 10485568 | bytes 230912 | tf_op jit(solution)/shard_map/while/body/eval_jaxpr/reduce_sum | solution.py:29
  93.8 0.1 fusion.56
  94.0 0.1 bitcast_multiply_fusion.3
  94.1 2.0 %fusion.58 = (f32[32]{0:T(128)S(1)}, f32[32]{0:T(128)S(1)}, f32[32]{0:T(128)S(1)}, f32[32]{0:T(128)S(1)}, f32[32]{0:T(128)S(1)}, /*index=5*/f32[32]{0:T(128)S(1)}) fusion(f32[32]{0:T(128)S(1)} %get-tuple-element.206, f32[8192]{0:T(1024)S(1)} %bitcast.131, f32[32]{0:T(128)S(1)} %get-tuple-element.208, f32[8192]{0:T(1024)S(1)} %bitcast.133, ...), kind=kLoop, calls=%fused_computation.25.clone.1 | loop fusion | flops 10485568 | bytes 230912 | tf_op jit(solution)/shard_map/while/body/eval_jaxpr/reduce_sum | solution.py:29
  96.2 0.1 fusion.56
  96.4 2.0 %fusion.58 = (f32[32]{0:T(128)S(1)}, f32[32]{0:T(128)S(1)}, f32[32]{0:T(128)S(1)}, f32[32]{0:T(128)S(1)}, f32[32]{0:T(128)S(1)}, /*index=5*/f32[32]{0:T(128)S(1)}) fusion(f32[32]{0:T(128)S(1)} %get-tuple-element.206, f32[8192]{0:T(1024)S(1)} %bitcast.131, f32[32]{0:T(128)S(1)} %get-tuple-element.208, f32[8192]{0:T(1024)S(1)} %bitcast.133, ...), kind=kLoop, calls=%fused_computation.25.clone.1 | loop fusion | flops 10485568 | bytes 230912 | tf_op jit(solution)/shard_map/while/body/eval_jaxpr/reduce_sum | solution.py:29
  98.5 0.1 fusion.56
  98.7 2.0 %fusion.58 = (f32[32]{0:T(128)S(1)}, f32[32]{0:T(128)S(1)}, f32[32]{0:T(128)S(1)}, f32[32]{0:T(128)S(1)}, f32[32]{0:T(128)S(1)}, /*index=5*/f32[32]{0:T(128)S(1)}) fusion(f32[32]{0:T(128)S(1)} %get-tuple-element.206, f32[8192]{0:T(1024)S(1)} %bitcast.131, f32[32]{0:T(128)S(1)} %get-tuple-element.208, f32[8192]{0:T(1024)S(1)} %bitcast.133, ...), kind=kLoop, calls=%fused_computation.25.clone.1 | loop fusion | flops 10485568 | bytes 230912 | tf_op jit(solution)/shard_map/while/body/eval_jaxpr/reduce_sum | solution.py:29
  100.8 0.8 copy.119
  101.6 0.3 slice_reduce_fusion.1
  101.8 2.0 %fusion.29 = (f32[32]{0:T(128)S(1)}, f32[32]{0:T(128)S(1)}, f32[32]{0:T(128)S(1)}, f32[32]{0:T(128)S(1)}, f32[32]{0:T(128)S(1)}, /*index=5*/f32[32]{0:T(128)S(1)}) fusion(f32[32]{0:T(128)S(1)} %get-tuple-element.111, f32[8192]{0:T(1024)S(1)} %bitcast.141, f32[32]{0:T(128)S(1)} %get-tuple-element.108, f32[8192]{0:T(1024)S(1)} %bitcast.143, ...), kind=kLoop, calls=%fused_computation.74 | loop fusion | flops 10485568 | bytes 230912 | tf_op jit(solution)/shard_map/reduce_sum | solution.py:29
  103.8 0.1 copy.113
  104.0 0.1 copy.115
  104.1 0.6 gather_fusion.2
  104.7 0.1 copy.114
  104.8 0.6 gather_fusion.3
  105.3 0.1 copy.116
  105.4 0.6 stack.52
  106.0 69.3 %reduce-scatter.4.cloned.1.call-done = f32[32,6]{1,0:T(8,128)} async-done(((f32[256,6]{1,0:T(8,128)}), f32[32,6]{1,0:T(8,128)}) %reduce-scatter.4.cloned.1.call-update) | async-done | bytes 784
  175.3 0.8 copy.118
  176.1 0.6 copy-done.1
  176.7 0.6 pad_maximum_fusion.2
  (68 shorter events, 1.2 us)
Async XLA Ops:
  7.2 168.2 %reduce-scatter.4.cloned.1.call-start = ((), (), s32[]{:S(2)}) async-start(), calls=%async_computation.1 | async-start | bytes 147456
  7.2 2.2 %copy-start.5 = (f32[3,256]{1,0:T(4,128)S(1)}, f32[3,256]{1,0:T(4,128)}, u32[]{:S(2)}) copy-start(f32[3,256]{1,0:T(4,128)} %param.14) | copy-start | bytes 9220
  7.9 1.5 copy-start.4
  7.9 1.5 copy-start.3
  8.7 0.7 copy-start.2
  8.7 0.7 copy-start
  9.5 0.7 copy-start.7
  11.4 0.7 copy-start.6
  176.1 0.6 copy-start.1
Sparse Core Ops, SparseCore 0:
  101.7 73.6 reduce-scatter.3
where the time goes:
time: 184 us
  blocking collectives  69.5 us (38%)
  waiting for transfers between devices  69.3 us (38%)
  other arithmetic  20.4 us (11%)
  between operations  14.9 us (8%)
  local copies, waits for them, and re-layouts  9.81 us (5%)
    unnamed x2, waiting for transfers between devices  69.3 us
    all_gather x1, blocking collectives, per_device(): group = lax.all_gather(block_data, 'grp', axis=1, tiled=True)  34.8 us
    all_gather x1, blocking collectives, per_device(): targets = lax.all_gather(own_set, 'blk', axis=1, tiled=True)  34.6 us
    reduce_sum x9, other arithmetic, pair_sums(): return jnp.stack([jnp.sum(scaled * term, axis=1) for term in term_list])  18 us
    unnamed x22, local copies, waits for them, and re-layouts  4.44 us
  transfers between devices with their start and end apart: 1, of which 1 were waited for; matrix products, arithmetic and copies ran while one was open for 2% of the time, Pallas kernels for 0%

commit v1 on v0

--- a/solution.py
+++ b/solution.py
@@ -51,7 +51,9 @@
     group = lax.all_gather(block_data, "grp", axis=1, tiled=True)
     group_src = group[:6]
     group_mass = group[6]
-    targets = lax.all_gather(own_set, "blk", axis=1, tiled=True)
+    targets = jnp.concatenate(
+        lax.all_to_all(jnp.stack([own_set] * lax.axis_size("blk")), "blk", 0, 0), axis=1
+    )
     blk_size = lax.axis_size("blk")
     blk_here = lax.axis_index("blk")
     block_total = group_src.shape[1] // BLOCK

time: 184 us -> 160 us (0.87)
  blocking collectives: 69.5 us -> 33.9 us
  starting transfers between devices: 0.04 us -> 6.97 us
    all_gather x1 -> x0, blocking collectives: 34.6 us -> none  [per_device(): targets = lax.all_gather(own_set, 'blk', axis=1, tiled=True)]
    all_to_all x0 -> x1, starting transfers between devices: none -> 6.93 us  [per_device(): lax.all_to_all(jnp.stack([own_set] * lax.axis_size('blk')), 'blk', 0, 0)]
    unnamed x22 -> x20, local copies, waits for them, and re-layouts: 4.44 us -> 5.55 us
  transfers between devices with their start and end apart: 1 -> 2, of which waited for: 1 -> 1; matrix products, arithmetic and copies ran while one was open for 2% -> 3% of each run, Pallas kernels for 0% -> 0%
where the time goes in v1:
time: 160 us
  waiting for transfers between devices  70.7 us (44%)
  blocking collectives  33.9 us (21%)
  other arithmetic  21.8 us (14%)
  between operations  14.8 us (9%)
  local copies, waits for them, and re-layouts  11.4 us (7%)
  starting transfers between devices  6.97 us (4%)
    unnamed x2, waiting for transfers between devices  70.6 us
    all_gather x1, blocking collectives, per_device(): group = lax.all_gather(block_data, 'grp', axis=1, tiled=True)  33.9 us
    reduce_sum x9, other arithmetic, pair_sums(): return jnp.stack([jnp.sum(scaled * term, axis=1) for term in term_list])  18 us
    all_to_all x1, starting transfers between devices, per_device(): lax.all_to_all(jnp.stack([own_set] * lax.axis_size('blk')), 'blk', 0, 0)  6.93 us
    unnamed x20, local copies, waits for them, and re-layouts  5.55 us
  transfers between devices with their start and end apart: 2, of which 1 were waited for; matrix products, arithmetic and copies ran while one was open for 3% of the time, Pallas kernels for 0%

profile of v1, /device:TPU:32, one launch (start us, length us, event | category | flops | bytes accessed | tf_op | source)
XLA Modules:
  0.0 160.0 jit_solution(12679471979992692837)
XLA Ops:
  7.2 0.7 broadcast_multiply_fusion
  7.9 0.7 multiply_add_fusion.1
  8.7 0.1 copy.91
  8.8 0.5 copy-done.5
  9.4 0.7 gather_fusion.1
  10.1 0.6 gather_fusion
  10.7 0.1 copy.92
  10.8 0.7 reshape.149
  11.5 6.9 %all-to-all-start = ((f32[8,1,192]{2,1,0:T(1,128)}), f32[8,1,192]{2,1,0:T(1,128)S(1)}, u32[]{:S(2)}, u32[]{:S(2)}) async-start(f32[8,1,192]{2,1,0:T(1,128)} %reshape.149), calls=%async_computation | async-start | bytes 16384 | tf_op jit(solution)/shard_map/all_to_all | solution.py:55
  19.2 0.6 copy-done.6
  19.8 0.1 fusion.36
  19.9 0.7 copy-done.4
  20.6 33.9 %all_gather.3 = f32[7,8192]{1,0:T(8,128)S(1)} all-gather(f32[7,256]{1,0:T(8,128)S(1)} %pad_maximum_fusion), channel_id=1, replica_groups=mesh['blk'=8,'grp'=32] {'grp'}, dimensions={1}, use_global_device_ids=true | all-gather | bytes 236544 | tf_op jit(solution)/shard_map/all_gather | solution.py:51
  54.6 0.2 fusion.44
  54.9 0.3 slice_reduce_fusion.1
  55.2 0.5 broadcast.150
  55.7 0.7 reduce.12
  56.4 18.5 %while.10 = (s32[]{:T(128)}, f32[8,6,32]{2,1,0:T(8,128)S(1)}, f32[8,64]{1,0:T(8,128)S(1)}, f32[1,8192]{1,0:T(1,128)S(1)}, f32[6,8192]{1,0:T(8,128)S(1)}, /*index=5*/f32[8,6,32]{2,1,0:T(8,128)S(1)}, s32[]{:T(128)}) while((s32[]{:T(128)}, f32[8,6,32]{2,1,0:T(8,128)S(1)}, f32[8,64]{1,0:T(8,128)S(1)}, f32[1,8192]{1,0:T(1,128)S(1)}, ...), condition=%wide.region_8.9_spmd, body=%wide.region_1.8_spmd.sunk | while | flops 10493762 | bytes 703321 | solution.py:74
  56.4 0.1 fusion.48
  56.7 2.0 %fusion.50 = (f32[32]{0:T(128)S(1)}, f32[32]{0:T(128)S(1)}, f32[32]{0:T(128)S(1)}, f32[32]{0:T(128)S(1)}, f32[32]{0:T(128)S(1)}, /*index=5*/f32[32]{0:T(128)S(1)}) fusion(f32[32]{0:T(128)S(1)} %get-tuple-element.171, f32[8192]{0:T(1024)S(1)} %bitcast.113, f32[32]{0:T(128)S(1)} %get-tuple-element.173, f32[8192]{0:T(1024)S(1)} %bitcast.115, ...), kind=kLoop, calls=%fused_computation.25.clone.1 | loop fusion | flops 10485568 | bytes 230912 | tf_op jit(solution)/shard_map/while/body/eval_jaxpr/reduce_sum | solution.py:29
  58.7 0.1 fusion.48
  59.0 2.0 %fusion.50 = (f32[32]{0:T(128)S(1)}, f32[32]{0:T(128)S(1)}, f32[32]{0:T(128)S(1)}, f32[32]{0:T(128)S(1)}, f32[32]{0:T(128)S(1)}, /*index=5*/f32[32]{0:T(128)S(1)}) fusion(f32[32]{0:T(128)S(1)} %get-tuple-element.171, f32[8192]{0:T(1024)S(1)} %bitcast.113, f32[32]{0:T(128)S(1)} %get-tuple-element.173, f32[8192]{0:T(1024)S(1)} %bitcast.115, ...), kind=kLoop, calls=%fused_computation.25.clone.1 | loop fusion | flops 10485568 | bytes 230912 | tf_op jit(solution)/shard_map/while/body/eval_jaxpr/reduce_sum | solution.py:29
  61.1 0.1 fusion.48
  61.3 2.0 %fusion.50 = (f32[32]{0:T(128)S(1)}, f32[32]{0:T(128)S(1)}, f32[32]{0:T(128)S(1)}, f32[32]{0:T(128)S(1)}, f32[32]{0:T(128)S(1)}, /*index=5*/f32[32]{0:T(128)S(1)}) fusion(f32[32]{0:T(128)S(1)} %get-tuple-element.171, f32[8192]{0:T(1024)S(1)} %bitcast.113, f32[32]{0:T(128)S(1)} %get-tuple-element.173, f32[8192]{0:T(1024)S(1)} %bitcast.115, ...), kind=kLoop, calls=%fused_computation.25.clone.1 | loop fusion | flops 10485568 | bytes 230912 | tf_op jit(solution)/shard_map/while/body/eval_jaxpr/reduce_sum | solution.py:29
  63.4 0.1 fusion.48
  63.6 2.0 %fusion.50 = (f32[32]{0:T(128)S(1)}, f32[32]{0:T(128)S(1)}, f32[32]{0:T(128)S(1)}, f32[32]{0:T(128)S(1)}, f32[32]{0:T(128)S(1)}, /*index=5*/f32[32]{0:T(128)S(1)}) fusion(f32[32]{0:T(128)S(1)} %get-tuple-element.171, f32[8192]{0:T(1024)S(1)} %bitcast.113, f32[32]{0:T(128)S(1)} %get-tuple-element.173, f32[8192]{0:T(1024)S(1)} %bitcast.115, ...), kind=kLoop, calls=%fused_computation.25.clone.1 | loop fusion | flops 10485568 | bytes 230912 | tf_op jit(solution)/shard_map/while/body/eval_jaxpr/reduce_sum | solution.py:29
  65.7 0.1 fusion.48
  65.9 2.0 %fusion.50 = (f32[32]{0:T(128)S(1)}, f32[32]{0:T(128)S(1)}, f32[32]{0:T(128)S(1)}, f32[32]{0:T(128)S(1)}, f32[32]{0:T(128)S(1)}, /*index=5*/f32[32]{0:T(128)S(1)}) fusion(f32[32]{0:T(128)S(1)} %get-tuple-element.171, f32[8192]{0:T(1024)S(1)} %bitcast.113, f32[32]{0:T(128)S(1)} %get-tuple-element.173, f32[8192]{0:T(1024)S(1)} %bitcast.115, ...), kind=kLoop, calls=%fused_computation.25.clone.1 | loop fusion | flops 10485568 | bytes 230912 | tf_op jit(solution)/shard_map/while/body/eval_jaxpr/reduce_sum | solution.py:29
  68.0 0.1 fusion.48
  68.3 2.0 %fusion.50 = (f32[32]{0:T(128)S(1)}, f32[32]{0:T(128)S(1)}, f32[32]{0:T(128)S(1)}, f32[32]{0:T(128)S(1)}, f32[32]{0:T(128)S(1)}, /*index=5*/f32[32]{0:T(128)S(1)}) fusion(f32[32]{0:T(128)S(1)} %get-tuple-element.171, f32[8192]{0:T(1024)S(1)} %bitcast.113, f32[32]{0:T(128)S(1)} %get-tuple-element.173, f32[8192]{0:T(1024)S(1)} %bitcast.115, ...), kind=kLoop, calls=%fused_computation.25.clone.1 | loop fusion | flops 10485568 | bytes 230912 | tf_op jit(solution)/shard_map/while/body/eval_jaxpr/reduce_sum | solution.py:29
  70.4 0.1 fusion.48
  70.6 2.0 %fusion.50 = (f32[32]{0:T(128)S(1)}, f32[32]{0:T(128)S(1)}, f32[32]{0:T(128)S(1)}, f32[32]{0:T(128)S(1)}, f32[32]{0:T(128)S(1)}, /*index=5*/f32[32]{0:T(128)S(1)}) fusion(f32[32]{0:T(128)S(1)} %get-tuple-element.171, f32[8192]{0:T(1024)S(1)} %bitcast.113, f32[32]{0:T(128)S(1)} %get-tuple-element.173, f32[8192]{0:T(1024)S(1)} %bitcast.115, ...), kind=kLoop, calls=%fused_computation.25.clone.1 | loop fusion | flops 10485568 | bytes 230912 | tf_op jit(solution)/shard_map/while/body/eval_jaxpr/reduce_sum | solution.py:29
  72.7 0.1 fusion.48
  72.9 2.0 %fusion.50 = (f32[32]{0:T(128)S(1)}, f32[32]{0:T(128)S(1)}, f32[32]{0:T(128)S(1)}, f32[32]{0:T(128)S(1)}, f32[32]{0:T(128)S(1)}, /*index=5*/f32[32]{0:T(128)S(1)}) fusion(f32[32]{0:T(128)S(1)} %get-tuple-element.171, f32[8192]{0:T(1024)S(1)} %bitcast.113, f32[32]{0:T(128)S(1)} %get-tuple-element.173, f32[8192]{0:T(1024)S(1)} %bitcast.115, ...), kind=kLoop, calls=%fused_computation.25.clone.1 | loop fusion | flops 10485568 | bytes 230912 | tf_op jit(solution)/shard_map/while/body/eval_jaxpr/reduce_sum | solution.py:29
  75.0 0.8 copy.100
  75.8 2.0 %fusion.23 = (f32[32]{0:T(128)S(1)}, f32[32]{0:T(128)S(1)}, f32[32]{0:T(128)S(1)}, f32[32]{0:T(128)S(1)}, f32[32]{0:T(128)S(1)}, /*index=5*/f32[32]{0:T(128)S(1)}) fusion(f32[32]{0:T(128)S(1)} %get-tuple-element.74, f32[8192]{0:T(1024)S(1)} %bitcast.122, f32[32]{0:T(128)S(1)} %get-tuple-element.76, f32[8192]{0:T(1024)S(1)} %bitcast.124, ...), kind=kLoop, calls=%fused_computation.69 | loop fusion | flops 10485568 | bytes 230912 | tf_op jit(solution)/shard_map/reduce_sum | solution.py:29
  77.8 0.1 copy.94
  77.9 0.5 copy-done.3
  78.5 0.1 copy.96
  78.6 0.6 gather_fusion.2
  79.2 0.1 copy.95
  79.2 0.6 gather_fusion.3
  79.8 0.1 copy.97
  79.9 0.6 stack.64
  80.5 70.6 %reduce-scatter.4.cloned.1.call-done = f32[32,6]{1,0:T(8,128)} async-done(((f32[256,6]{1,0:T(8,128)}), f32[32,6]{1,0:T(8,128)}) %reduce-scatter.4.cloned.1.call-update) | async-done | bytes 784
  151.2 0.8 copy.99
  152.0 0.6 copy-done.1
  152.6 0.6 pad_maximum_fusion.2
  (77 shorter events, 1.5 us)
Async XLA Ops:
  7.2 0.8 copy-start
  8.7 0.7 copy-start.5
  11.5 43.6 %all-to-all-start = ((f32[8,1,192]{2,1,0:T(1,128)}), f32[8,1,192]{2,1,0:T(1,128)S(1)}, u32[]{:S(2)}, u32[]{:S(2)}) async-start(f32[8,1,192]{2,1,0:T(1,128)} %reshape.149), calls=%async_computation | async-start | bytes 16384 | tf_op jit(solution)/shard_map/all_to_all | solution.py:55
  18.4 132.7 %reduce-scatter.4.cloned.1.call-start = ((), (), s32[]{:S(2)}) async-start(), calls=%async_computation.2 | async-start | bytes 147456
  19.1 0.7 copy-start.6
  19.9 0.7 copy-start.4
  75.7 2.0 %copy-start.2 = (f32[3,256]{1,0:T(4,128)S(1)}, f32[3,256]{1,0:T(4,128)}, u32[]{:S(2)}) copy-start(f32[3,256]{1,0:T(4,128)} %param.15) | copy-start | bytes 9220
  77.8 0.7 copy-start.3
  151.9 0.6 copy-start.1
Sparse Core Ops, SparseCore 0:
  75.9 75.2 reduce-scatter.3
